TPU v7x, 256 devices: a whole 4x4x8 slice. The times are simulated.
256 devices in a mesh: rows: 16 (over x, y), sub: 16 (over z, core).
Axes of the slice: x: 4, y: 4, z: 8, core: 2. Of those that a mesh axis runs over, the one named last changes fastest.
Arguments:
- embeddings: bfloat16 [65536, 1024], P(('rows', 'sub'))
- codes: int32 [64, 65536], P(None, ('rows', 'sub')), may hold values from 0 to 255
- codebook: bfloat16 [256, 1024], P(None, 'sub'), may hold values from -6 to 6
Outputs:
- rotation: float32 [1024, 1024], P('sub')
- rotated: bfloat16 [65536, 1024], P(('rows', 'sub'))
- new_codebook: float32 [256, 1024], P(None, 'sub')
All inputs are finite; a program needn't handle non-finite values.
Results may differ from a plain program's by a relative error of at most 0.0095.
Values may be sent and summed in bfloat16 or wider, within the bound.
No kernel may reach another device: no remote copies, remote signals or barrier semaphores. Data moves between devices by JAX's collectives and lax.ppermute only.
A program may use at most 64 MiB of HBM per device.

v0:
```python
import jax
import jax.numpy as jnp
from jax import lax
from jax.sharding import PartitionSpec as P

NS_STEPS = 3
coef_a = 3.4445
coef_b = -4.775
coef_c = 2.0315
frob_eps = 1e-07


def one_hot_codes(code_block, count_codes):
    levels = lax.broadcasted_iota(jnp.int32, code_block.shape + (count_codes,), 2)
    return (code_block[:, :, None] == levels).astype(jnp.bfloat16)


def decode_rows(codes, table):
    subspaces, local_rows = codes.shape
    count_codes, row_width = table.shape
    sub_width = row_width // subspaces
    codewords = table.reshape(count_codes, subspaces, sub_width)
    one_hot = one_hot_codes(codes, count_codes)
    picked = jnp.einsum("mnk,kmj->nmj", one_hot, codewords, preferred_element_type=jnp.float32)
    return picked.reshape(local_rows, row_width).astype(jnp.bfloat16)


def codeword_sums(codes, row_values, count_codes):
    subspaces, local_rows = codes.shape
    row_width = row_values.shape[1]
    sub_width = row_width // subspaces
    one_hot = one_hot_codes(codes, count_codes)
    pieces = row_values.reshape(local_rows, subspaces, sub_width)
    code_sums = jnp.einsum("mnk,nmj->kmj", one_hot, pieces, preferred_element_type=jnp.float32)
    return code_sums.reshape(count_codes, row_width)


def rows_sum(x):
    groups = lax.axis_size("rows")
    chunk = x.shape[0] // groups
    scattered = lax.all_to_all(x, "rows", split_axis=0, concat_axis=0, tiled=True)
    own = jnp.sum(scattered.reshape((groups, chunk) + x.shape[1:]), axis=0)
    spread = jnp.broadcast_to(own[None], (groups,) + own.shape).reshape(x.shape)
    return lax.all_to_all(spread, "rows", split_axis=0, concat_axis=0, tiled=True)


def panel_rows_sum(x):
    groups = lax.axis_size("rows")
    height, width = x.shape
    tiles = (
        x.reshape(height // 8, 8, 2, width // 2)
        .transpose(0, 2, 1, 3)
        .reshape(groups, 8, width // 2)
    )
    scattered = lax.all_to_all(tiles, "rows", split_axis=0, concat_axis=0, tiled=True)
    own = jnp.sum(scattered, axis=0)
    spread = jnp.broadcast_to(own[None], scattered.shape)
    gathered = lax.all_to_all(spread, "rows", split_axis=0, concat_axis=0, tiled=True)
    return (
        gathered.reshape(height // 8, 2, 8, width // 2).transpose(0, 2, 1, 3).reshape(height, width)
    )


def bdot(left, right, dims):
    return lax.dot_general(
        left.astype(jnp.bfloat16),
        right.astype(jnp.bfloat16),
        (dims, ((), ())),
        preferred_element_type=jnp.float32,
    )


def partner(x):
    count = lax.axis_size("sub")
    return lax.ppermute(x, "sub", [(i, i ^ 1) for i in range(count)])


def newton_half(z_own, z_other_half):
    own_half = z_own.astype(jnp.bfloat16)
    gram_own = bdot(own_half, own_half, ((1,), (1,)))
    gram_cross = bdot(own_half, z_other_half, ((1,), (1,)))
    gram_other = partner(gram_own.astype(jnp.bfloat16))
    own_block, cross_block = (gram_own.astype(jnp.bfloat16), gram_cross.astype(jnp.bfloat16))
    gram_rows = jnp.concatenate([own_block, cross_block], axis=1)
    quartic_left = bdot(gram_rows, gram_rows, ((1,), (1,)))
    quartic_right = bdot(own_block, cross_block, ((1,), (0,))) + bdot(
        cross_block, gram_other, ((1,), (0,))
    )
    mixer = jnp.concatenate(
        [coef_b * gram_own + coef_c * quartic_left, coef_b * gram_cross + coef_c * quartic_right],
        axis=1,
    )
    local_rows = jnp.concatenate([own_half, z_other_half], axis=0)
    return coef_a * z_own + bdot(mixer, local_rows, ((1,), (0,)))


def body(embeddings, codes, codebook):
    moved_codes = lax.all_to_all(codes, "sub", split_axis=0, concat_axis=1, tiled=True)
    table = lax.all_gather(codebook, "sub", axis=1, tiled=True)
    decoded = decode_rows(codes, table)
    partial_t = lax.dot_general(
        decoded, embeddings, (((0,), (0,)), ((), ())), preferred_element_type=jnp.float32
    )
    partial_panel = lax.psum_scatter(partial_t, "sub", scatter_dimension=1, tiled=True).T
    code_one_hot = one_hot_codes(moved_codes, table.shape[0])
    counts = jnp.sum(code_one_hot, axis=1, dtype=jnp.float32).T
    core = lax.axis_index("sub") % 2
    panel_rows = partial_panel.shape[0]
    columns = embeddings.reshape(embeddings.shape[0], -1, 2, panel_rows)
    own_columns = lax.dynamic_index_in_dim(columns, core, axis=2, keepdims=False).reshape(
        embeddings.shape[0], -1
    )
    other_columns = lax.dynamic_index_in_dim(columns, 1 - core, axis=2, keepdims=False).reshape(
        embeddings.shape[0], -1
    )
    partial_panel, moved_codes, counts, own_columns, other_columns = lax.optimization_barrier(
        (partial_panel, moved_codes, counts, own_columns, other_columns)
    )
    cross_panel = panel_rows_sum(partial_panel)
    cross = lax.all_gather(cross_panel, "sub", axis=0, tiled=True)
    width = cross.shape[1]
    frob_scale = jnp.sqrt(jnp.sum(cross * cross)) + frob_eps
    core = lax.axis_index("sub") % 2
    panel_rows = cross.shape[0] // lax.axis_size("sub")
    by_parity = cross.reshape(-1, 2, panel_rows, width)
    z_own = (
        lax.dynamic_index_in_dim(by_parity, core, axis=1, keepdims=False).reshape(-1, width)
        / frob_scale
    )
    z_other = (
        lax.dynamic_index_in_dim(by_parity, 1 - core, axis=1, keepdims=False).reshape(-1, width)
        / frob_scale
    )
    z_other_half = z_other.astype(jnp.bfloat16)
    for newton_step_index in range(NS_STEPS - 1):
        z_own = newton_half(z_own, z_other_half)
        z_other_half = partner(z_own.astype(jnp.bfloat16))
    z_own = newton_half(z_own, z_other_half)
    own_half = z_own.astype(jnp.bfloat16)
    z_other_half = partner(own_half)
    rotated = (
        jnp.dot(own_columns, own_half, preferred_element_type=jnp.float32)
        + jnp.dot(other_columns, z_other_half, preferred_element_type=jnp.float32)
    ).astype(jnp.bfloat16)
    moved_rows = lax.all_to_all(rotated, "sub", split_axis=1, concat_axis=0, tiled=True)
    code_sums = codeword_sums(moved_codes, moved_rows, table.shape[0])
    sums_width = code_sums.shape[1]
    padded_counts = jnp.pad(counts, ((0, 0), (0, sums_width - counts.shape[1])))
    totals = rows_sum(jnp.concatenate([code_sums, padded_counts], axis=1))
    code_sums, counts = (
        totals[:, :sums_width],
        totals[:, sums_width : sums_width + counts.shape[1]],
    )
    own_codebook = codebook.astype(jnp.float32)
    spread = jnp.repeat(counts, own_codebook.shape[1] // counts.shape[1], axis=1)
    new_codebook = (code_sums + own_codebook) / (spread + 1.0)
    me = lax.axis_index("sub")
    panel = lax.dynamic_index_in_dim(
        z_own.reshape(-1, panel_rows, width), me // 2, axis=0, keepdims=False
    )
    return (panel, rotated, new_codebook)


def solution(mesh):
    in_specs = (P(("rows", "sub"), None), P(None, ("rows", "sub")), P(None, "sub"))
    out_specs = (P("sub", None), P(("rows", "sub"), None), P(None, "sub"))
    return jax.shard_map(body, mesh=mesh, in_specs=in_specs, out_specs=out_specs, check_vma=False)
```

profile of v0, /device:TPU:1, one launch (start us, length us, event | category | flops | bytes accessed | tf_op | source)
XLA Modules:
  0.0 252.7 jit_solution(4950489378078883166)
XLA Ops:
  7.2 23.0 %all_gather.6 = bf16[256,1024]{0,1:T(8,128)(2,1)S(1)} all-gather(bf16[256,64]{0,1:T(8,128)(2,1)} %param.5), channel_id=1, replica_groups=mesh['rows'=16,'sub'=16] {'sub'}, dimensions={1}, use_global_device_ids=true | all-gather | bytes 557056 | tf_op jit(solution)/shard_map/all_gather | solution.py:99
  30.2 5.3 %fusion.29 = bf16[64,256,16]{1,2,0:T(8,128)(2,1)S(1)} fusion(bf16[256,64,16]{0,2,1:T(8,128)(2,1)S(1)} %bitcast.89, s32[64,256]{1,0:T(8,128)} %param.4), kind=kOutput, calls=%fused_computation.42 | convolution fusion | flops 138674176 | bytes 1114112 | tf_op jit(solution)/shard_map/mnk,kmj->nmj/dot_general | solution.py:24
  35.5 2.7 %fusion.74 = f32[1024,1024]{0,1:T(8,128)} fusion(bf16[256,1024]{0,1:T(8,128)(2,1)S(1)} %bitcast.82, bf16[256,1024]{1,0:T(8,128)(2,1)S(1)} %copy-done), kind=kOutput, calls=%fused_computation.92 | convolution fusion | flops 536870912 | bytes 5242880 | tf_op jit(solution)/shard_map/dot_general | solution.py:101
  38.3 0.8 copy-done.3
  39.1 0.6 all_to_all.42
  39.8 3.8 %all-to-all-start = ((s32[16,4,256]{2,1,0:T(4,128)}), s32[16,4,256]{2,1,0:T(4,128)S(1)}, u32[]{:S(2)}, u32[]{:S(2)}) async-start(s32[16,4,256]{2,1,0:T(4,128)} %all_to_all.42), calls=%async_computation.1 | async-start | bytes 131072 | tf_op jit(solution)/shard_map/all_to_all | solution.py:98
  43.6 0.2 copy.42
  43.9 7.5 %all-to-all-done = s32[16,4,256]{2,1,0:T(4,128)S(1)} async-done(((s32[16,4,256]{2,1,0:T(4,128)}), s32[16,4,256]{2,1,0:T(4,128)S(1)}, u32[]{:S(2)}, u32[]{:S(2)}) %all-to-all-start) | async-done | bytes 65568 | tf_op jit(solution)/shard_map/all_to_all | solution.py:98
  51.4 6.9 %convert_reduce_fusion = f32[4,256]{1,0:T(4,128)S(1)} fusion(s32[4,4096]{1,0:T(4,128)S(1)} %bitcast.92), kind=kLoop, calls=%fused_computation.1 | loop fusion | flops 16776192 | bytes 69632 | tf_op jit(solution)/shard_map/reduce_sum | solution.py:106
  58.3 37.9 %reduce-scatter.2.cloned.1.call-done = f32[1024,64]{0,1:T(8,128)} async-done(((f32[1024,1024]{0,1:T(8,128)}), f32[1024,64]{0,1:T(8,128)}) %reduce-scatter.2.cloned.1.call-update) | async-done | bytes 262160 | tf_op jit(solution)/shard_map/reduce_scatter | solution.py:104
  96.3 13.8 %all_to_all.60 = f32[16,8,512]{2,1,0:T(8,128)S(1)} all-to-all(f32[16,8,512]{2,1,0:T(8,128)} %bitcast.91), channel_id=1, replica_groups=mesh['rows'=16,'sub'=16] {'rows'}, dimensions={0} | all-to-all | bytes 524288 | tf_op jit(solution)/shard_map/all_to_all | solution.py:55
  110.1 10.6 %all_to_all.61 = f32[16,8,512]{2,1,0:T(8,128)} all-to-all(f32[16,8,512]{2,1,0:T(8,128)S(1)} %broadcast_in_dim.6), channel_id=1, replica_groups=mesh['rows'=16,'sub'=16] {'rows'}, dimensions={0} | all-to-all | bytes 524288 | tf_op jit(solution)/shard_map/all_to_all | solution.py:58
  120.8 43.7 %all-gather.2.cloned.1.call-done = f32[1024,1024]{1,0:T(8,128)} async-done(((f32[64,1024]{1,0:T(8,128)}), f32[1024,1024]{1,0:T(8,128)}) %all-gather.2.cloned.1.call-update) | async-done | bytes 4194320 | tf_op jit(solution)/shard_map/all_gather | solution.py:120
  164.5 3.9 %multiply_reduce_fusion = f32[]{:T(128)} fusion(f32[1024,1024]{1,0:T(8,128)} %all-gather.2.cloned.1.call-done), kind=kLoop, calls=%fused_computation.9 | loop fusion | flops 2097151 | bytes 4194308 | tf_op jit(solution)/shard_map/reduce_sum | solution.py:122
  169.1 2.9 %fusion.57 = (bf16[8,1,64,1024]{3,2,1,0:T(8,128)(2,1)S(1)}, bf16[8,1,64,1024]{3,2,1,0:T(8,128)(2,1)S(1)}, f32[8,1,64,1024]{3,2,1,0:T(8,128)S(1)}) fusion(f32[]{:T(128)S(6)} %add.83, f32[8,2,64,1024]{3,2,1,0:T(8,128)} %bitcast.76, s32[]{:T(128)S(6)} %select_n.28, s32[]{:T(128)S(6)} %select_n.29), kind=kLoop, calls=%fused_computation.69 | loop fusion | flops 2621440 | bytes 8388620 | tf_op jit(solution)/shard_map/convert_element_type | solution.py:79
  171.9 0.7 fusion.66
  172.7 0.7 fusion.65
  173.4 0.4 collective-permute-start
  173.8 0.8 fusion.30
  174.6 0.4 fusion.76
  175.0 0.4 collective-permute-done
  175.4 0.5 fusion.33
  175.9 1.3 fusion.67
  177.2 0.4 collective-permute-start.1
  177.6 0.7 fusion.69
  178.4 0.5 collective-permute-start.2
  178.8 1.1 collective-permute-done.1
  180.0 0.7 fusion.68
  180.7 0.8 fusion.31
  181.5 0.4 fusion.77
  181.9 0.5 add_convert_fusion.1
  182.5 1.3 fusion.70
  183.7 0.4 collective-permute-start.3
  184.1 0.7 fusion.72
  184.9 0.3 collective-permute-start.4
  185.2 1.3 collective-permute-done.3
  186.5 0.7 fusion.71
  187.2 0.8 fusion.32
  188.0 0.4 fusion.78
  188.4 0.5 add_convert_fusion
  189.0 1.3 fusion.73
  190.2 0.4 collective-permute-start.5
  190.6 0.5 fusion.75
  191.1 1.9 collective-permute-done.5
  193.0 0.5 fusion.28
  193.5 1.0 copy.43
  194.5 4.6 %all-to-all-start.3 = ((bf16[256,16,64]{0,2,1:T(8,128)(2,1)}), bf16[256,16,64]{0,2,1:T(8,128)(2,1)S(1)}, u32[]{:S(2)}, u32[]{:S(2)}) async-start(bf16[256,16,64]{0,2,1:T(8,128)(2,1)} %bitcast.23), calls=%async_computation.4 | async-start | bytes 1048576 | tf_op jit(solution)/shard_map/all_to_all | solution.py:145
  199.1 0.1 copy.55
  199.2 17.0 %all-to-all-done.3 = bf16[256,16,64]{0,2,1:T(8,128)(2,1)S(1)} async-done(((bf16[256,16,64]{0,2,1:T(8,128)(2,1)}), bf16[256,16,64]{0,2,1:T(8,128)(2,1)S(1)}, u32[]{:S(2)}, u32[]{:S(2)}) %all-to-all-start.3) | async-done | bytes 524320 | tf_op jit(solution)/shard_map/all_to_all | solution.py:145
  216.3 0.3 copy.44
  216.6 0.2 reshape.97
  216.8 3.2 %fusion.34 = f32[256,4,16]{0,2,1:T(8,128)S(1)} fusion(bf16[4096,4,16]{0,2,1:T(8,128)(2,1)S(1)} %reshape.97, s32[4,4096]{1,0:T(4,128)S(1)} %bitcast.93), kind=kOutput, calls=%fused_computation.47 | convolution fusion | flops 138412032 | bytes 655360 | tf_op jit(solution)/shard_map/mnk,nmj->kmj/dot_general | solution.py:34
  220.0 0.2 concatenate.47
  220.2 0.2 copy.46
  220.5 0.1 pad_maximum_fusion
  220.6 13.3 %all_to_all.62 = f32[16,16,128]{2,1,0:T(8,128)S(1)} all-to-all(f32[16,16,128]{2,1,0:T(8,128)S(1)} %pad_maximum_fusion), channel_id=1, replica_groups=mesh['rows'=16,'sub'=16] {'rows'}, dimensions={0} | all-to-all | bytes 262144 | tf_op jit(solution)/shard_map/all_to_all | solution.py:41
  233.9 0.7 broadcast_in_dim.7
  234.6 3.5 %all-to-all-start.5 = ((f32[16,16,128]{2,1,0:T(8,128)}), f32[16,16,128]{2,1,0:T(8,128)S(1)}, u32[]{:S(2)}, u32[]{:S(2)}) async-start(f32[16,16,128]{2,1,0:T(8,128)} %broadcast_in_dim.7), calls=%async_computation.6 | async-start | bytes 262144 | tf_op jit(solution)/shard_map/all_to_all | solution.py:44
  238.2 0.1 copy.49
  238.3 0.7 dynamic-slice_bitcast_fusion
  239.0 5.8 %all-to-all-done.5 = f32[16,16,128]{2,1,0:T(8,128)S(1)} async-done(((f32[16,16,128]{2,1,0:T(8,128)}), f32[16,16,128]{2,1,0:T(8,128)S(1)}, u32[]{:S(2)}, u32[]{:S(2)}) %all-to-all-start.5) | async-done | bytes 131104 | tf_op jit(solution)/shard_map/all_to_all | solution.py:44
  244.9 0.1 slice.9
  245.1 0.1 copy.51
  245.2 0.7 copy.52
  (22 shorter events, 0.4 us)
Async XLA Ops:
  7.2 89.1 %reduce-scatter.2.cloned.1.call-start = ((), (), s32[]{:S(2)}) async-start(), calls=%async_computation.7 | async-start | bytes 4456448 | tf_op jit(solution)/shard_map/reduce_scatter | solution.py:104
  30.2 5.3 %copy-start = (bf16[256,1024]{1,0:T(8,128)(2,1)S(1)}, bf16[256,1024]{1,0:T(8,128)(2,1)}, u32[]{:S(2)}) copy-start(bf16[256,1024]{1,0:T(8,128)(2,1)} %param.3) | copy-start | bytes 1572868
  38.3 0.8 copy-start.3
  39.8 11.7 %all-to-all-start = ((s32[16,4,256]{2,1,0:T(4,128)}), s32[16,4,256]{2,1,0:T(4,128)S(1)}, u32[]{:S(2)}, u32[]{:S(2)}) async-start(s32[16,4,256]{2,1,0:T(4,128)} %all_to_all.42), calls=%async_computation.1 | async-start | bytes 131072 | tf_op jit(solution)/shard_map/all_to_all | solution.py:98
  43.6 120.9 %all-gather.2.cloned.1.call-start = ((), (), s32[]{:S(2)}) async-start(), calls=%async_computation.8 | async-start | bytes 4456448 | tf_op jit(solution)/shard_map/all_gather | solution.py:120
  173.4 2.0 collective-permute-start
  177.2 2.7 %collective-permute-start.1 = (bf16[512,1024]{1,0:T(8,128)(2,1)S(1)}, bf16[512,1024]{1,0:T(8,128)(2,1)S(1)}, u32[]{:S(2)}, u32[]{:S(2)}) collective-permute-start(bf16[512,1024]{1,0:T(8,128)(2,1)S(1)} %get-tuple-element.37), channel_id=1, source_target_pairs={{0,1},{1,0},{2,3},{3,2},{4,5},{5,4},{6,7},{7,6},{8,9},{9,8},{10,11... | collective-permute-start | bytes 3145736 | tf_op jit(solution)/shard_map/ppermute | solution.py:75
  178.4 3.6 %collective-permute-start.2 = (bf16[512,512]{0,1:T(8,128)(2,1)S(1)}, bf16[512,512]{0,1:T(8,128)(2,1)S(1)}, u32[]{:S(2)}, u32[]{:S(2)}) collective-permute-start(bf16[512,512]{0,1:T(8,128)(2,1)S(1)} %get-tuple-element.41), channel_id=1, source_target_pairs={{0,1},{1,0},{2,3},{3,2},{4,5},{5,4},{6,7},{7,6},{8,9},{9,8},{10,11... | collective-permute-start | bytes 1572872 | tf_op jit(solution)/shard_map/ppermute | solution.py:75
  183.7 2.7 %collective-permute-start.3 = (bf16[512,1024]{1,0:T(8,128)(2,1)S(1)}, bf16[512,1024]{1,0:T(8,128)(2,1)S(1)}, u32[]{:S(2)}, u32[]{:S(2)}) collective-permute-start(bf16[512,1024]{1,0:T(8,128)(2,1)S(1)} %get-tuple-element.43), channel_id=1, source_target_pairs={{0,1},{1,0},{2,3},{3,2},{4,5},{5,4},{6,7},{7,6},{8,9},{9,8},{10,11... | collective-permute-start | bytes 3145736 | tf_op jit(solution)/shard_map/ppermute | solution.py:75
  184.9 3.6 %collective-permute-start.4 = (bf16[512,512]{0,1:T(8,128)(2,1)S(1)}, bf16[512,512]{0,1:T(8,128)(2,1)S(1)}, u32[]{:S(2)}, u32[]{:S(2)}) collective-permute-start(bf16[512,512]{0,1:T(8,128)(2,1)S(1)} %get-tuple-element.47), channel_id=1, source_target_pairs={{0,1},{1,0},{2,3},{3,2},{4,5},{5,4},{6,7},{7,6},{8,9},{9,8},{10,11... | collective-permute-start | bytes 1572872 | tf_op jit(solution)/shard_map/ppermute | solution.py:75
  190.2 2.7 %collective-permute-start.5 = (bf16[512,1024]{1,0:T(8,128)(2,1)S(1)}, bf16[512,1024]{1,0:T(8,128)(2,1)S(1)}, u32[]{:S(2)}, u32[]{:S(2)}) collective-permute-start(bf16[512,1024]{1,0:T(8,128)(2,1)S(1)} %get-tuple-element.49), channel_id=1, source_target_pairs={{0,1},{1,0},{2,3},{3,2},{4,5},{5,4},{6,7},{7,6},{8,9},{9,8},{10,11... | collective-permute-start | bytes 3145736 | tf_op jit(solution)/shard_map/ppermute | solution.py:75
  193.4 1.0 copy-start.1
  194.5 21.8 %all-to-all-start.3 = ((bf16[256,16,64]{0,2,1:T(8,128)(2,1)}), bf16[256,16,64]{0,2,1:T(8,128)(2,1)S(1)}, u32[]{:S(2)}, u32[]{:S(2)}) async-start(bf16[256,16,64]{0,2,1:T(8,128)(2,1)} %bitcast.23), calls=%async_computation.4 | async-start | bytes 1048576 | tf_op jit(solution)/shard_map/all_to_all | solution.py:145
  220.0 18.1 %copy-start.2 = (bf16[256,64]{0,1:T(8,128)(2,1)S(1)}, bf16[256,64]{0,1:T(8,128)(2,1)}, u32[]{:S(2)}) copy-start(bf16[256,64]{0,1:T(8,128)(2,1)} %param.5) | copy-start | bytes 98308
  234.6 10.2 %all-to-all-start.5 = ((f32[16,16,128]{2,1,0:T(8,128)}), f32[16,16,128]{2,1,0:T(8,128)S(1)}, u32[]{:S(2)}, u32[]{:S(2)}) async-start(f32[16,16,128]{2,1,0:T(8,128)} %broadcast_in_dim.7), calls=%async_computation.6 | async-start | bytes 262144 | tf_op jit(solution)/shard_map/all_to_all | solution.py:44
Sparse Core Ops, SparseCore 0:
  38.4 57.8 reduce-scatter.1
  120.9 43.5 all-gather.1
where the time goes:
time: 254 us; the launch traced here: 253 us
  waiting for transfers between devices  117 us (46%)
  blocking collectives  60.8 us (24%)
  matrix products  25.6 us (10%)
  between operations  15.1 us (6%)
  starting transfers between devices  14.3 us (6%)
  other arithmetic  13.8 us (5%)
  local copies, waits for them, and re-layouts  6.4 us (3%)
    all_gather x1, waiting for transfers between devices, body(): cross = lax.all_gather(cross_panel, 'sub', axis=0, tiled=True)  43.7 us
    reduce_scatter x1, waiting for transfers between devices, body(): lax.psum_scatter(partial_t, 'sub', scatter_dimension=1, tiled=True)  37.9 us
    all_gather x1, blocking collectives, body(): table = lax.all_gather(codebook, 'sub', axis=1, tiled=True)  23 us
    all_to_all x1, waiting for transfers between devices, body(): lax.all_to_all(rotated, 'sub', split_axis=1, concat_axis=0, tiled=True)  17 us
    all_to_all x1, blocking collectives, panel_rows_sum(): lax.all_to_all(tiles, 'rows', split_axis=0, concat_axis=0, tiled=True)  13.8 us
    dot_general x18, matrix products, bdot(): lax.dot_general(left.astype(jnp.bfloat16), right.astype(jnp.bfloat16), (d...  13.4 us
    all_to_all x1, blocking collectives, rows_sum(): lax.all_to_all(x, 'rows', split_axis=0, concat_axis=0, tiled=True)  13.3 us
    all_to_all x1, blocking collectives, panel_rows_sum(): lax.all_to_all(spread, 'rows', split_axis=0, concat_axis=0, tiled=True)  10.6 us
  transfers between devices with their start and end apart: 11, of which 9 were waited for; matrix products, arithmetic and copies ran while one was open for 6% of the time, Pallas kernels for 0%

commit v1 on v0

--- a/solution.py
+++ b/solution.py
@@ -8,6 +8,22 @@
 coef_b = -4.775
 coef_c = 2.0315
 frob_eps = 1e-07
+
+
+def collect(x, axis, dim):
+    ways, here, step = (lax.axis_size(axis), lax.axis_index(axis), x.shape[dim])
+    lengths = [n * ways if d == dim else n for d, n in enumerate(x.shape)]
+    full = lax.dynamic_update_slice_in_dim(jnp.zeros(lengths, x.dtype), x, here * step, axis=dim)
+    going_up = going_down = x
+    for far in range(1, ways // 2 + 1):
+        going_up = lax.ppermute(going_up, axis, [(d, (d + 1) % ways) for d in range(ways)])
+        full = lax.dynamic_update_slice_in_dim(full, going_up, (here - far) % ways * step, axis=dim)
+        if 2 * far < ways:
+            going_down = lax.ppermute(going_down, axis, [(d, (d - 1) % ways) for d in range(ways)])
+            full = lax.dynamic_update_slice_in_dim(
+                full, going_down, (here + far) % ways * step, axis=dim
+            )
+    return full
 
 
 def one_hot_codes(code_block, count_codes):
@@ -96,7 +112,7 @@
 
 def body(embeddings, codes, codebook):
     moved_codes = lax.all_to_all(codes, "sub", split_axis=0, concat_axis=1, tiled=True)
-    table = lax.all_gather(codebook, "sub", axis=1, tiled=True)
+    table = collect(codebook, "sub", 1)
     decoded = decode_rows(codes, table)
     partial_t = lax.dot_general(
         decoded, embeddings, (((0,), (0,)), ((), ())), preferred_element_type=jnp.float32

time: 254 us -> 274 us (1.079)
  starting transfers between devices: 14.3 us -> 46.7 us
  blocking collectives: 60.8 us -> 37.8 us
  waiting for transfers between devices: 117 us -> 127 us
    ppermute x0 -> x15, starting transfers between devices: none -> 26.3 us  [the longest x7 20.4 us: collect(): lax.ppermute(going_down, axis, [(d, (d - 1) % ways) for d in range(ways)])]
    all_gather x1 -> x0, blocking collectives: 23 us -> none  [body(): table = lax.all_gather(codebook, 'sub', axis=1, tiled=True)]
    ppermute x0 -> x15, waiting for transfers between devices: none -> 9.46 us  [the longest x8 8.56 us: collect(): lax.ppermute(going_up, axis, [(d, (d + 1) % ways) for d in range(ways)])]
    all_to_all x1, starting transfers between devices: 3.8 us -> 9.97 us  [body(): lax.all_to_all(codes, 'sub', split_axis=0, concat_axis=1, tiled=True)]
  transfers between devices with their start and end apart: 11 -> 26, of which waited for: 9 -> 22; matrix products, arithmetic and copies ran while one was open for 6% -> 6% of each run, Pallas kernels for 0% -> 0%
where the time goes in v1:
time: 274 us; the launch traced here: 273 us
  waiting for transfers between devices  127 us (46%)
  starting transfers between devices  46.7 us (17%)
  blocking collectives  37.8 us (14%)
  matrix products  25.6 us (9%)
  between operations  15.1 us (6%)
  other arithmetic  13.8 us (5%)
  local copies, waits for them, and re-layouts  7.24 us (3%)
    all_gather x1, waiting for transfers between devices, body(): cross = lax.all_gather(cross_panel, 'sub', axis=0, tiled=True)  43.9 us
    reduce_scatter x1, waiting for transfers between devices, body(): lax.psum_scatter(partial_t, 'sub', scatter_dimension=1, tiled=True)  37.9 us
    ppermute x7, starting transfers between devices, collect(): lax.ppermute(going_down, axis, [(d, (d - 1) % ways) for d in range(ways)])  20.4 us
    all_to_all x1, waiting for transfers between devices, body(): lax.all_to_all(rotated, 'sub', split_axis=1, concat_axis=0, tiled=True)  17 us
    all_to_all x1, blocking collectives, panel_rows_sum(): lax.all_to_all(tiles, 'rows', split_axis=0, concat_axis=0, tiled=True)  13.8 us
    dot_general x18, matrix products, bdot(): lax.dot_general(left.astype(jnp.bfloat16), right.astype(jnp.bfloat16), (d...  13.4 us
    all_to_all x1, blocking collectives, rows_sum(): lax.all_to_all(x, 'rows', split_axis=0, concat_axis=0, tiled=True)  13.3 us
    all_to_all x1, blocking collectives, panel_rows_sum(): lax.all_to_all(spread, 'rows', split_axis=0, concat_axis=0, tiled=True)  10.6 us
  transfers between devices with their start and end apart: 26, of which 22 were waited for; matrix products, arithmetic and copies ran while one was open for 6% of the time, Pallas kernels for 0%

profile of v1, /device:TPU:1, one launch (start us, length us, event | category | flops | bytes accessed | tf_op | source)
XLA Modules:
  0.0 272.7 jit_solution(10190870518254151834)
XLA Ops:
  7.2 3.0 %collective-permute-start = (bf16[256,64]{0,1:T(8,128)(2,1)}, bf16[256,64]{0,1:T(8,128)(2,1)S(1)}, u32[]{:S(2)}, u32[]{:S(2)}) collective-permute-start(bf16[256,64]{0,1:T(8,128)(2,1)} %param.5), channel_id=1, source_target_pairs={{0,1},{1,2},{2,3},{3,4},{4,5},{5,6},{6,7},{7,8},{8,9},{9,10},{10,1... | collective-permute-start | bytes 98312 | tf_op jit(solution)/shard_map/ppermute | solution.py:19
  10.5 0.8 constant_dynamic-update-slice_fusion.15
  11.6 2.2 collective-permute-start.2
  13.8 2.2 collective-permute-start.3
  16.0 0.6 collective-permute-done.2
  16.5 0.6 collective-permute-start.4
  17.1 3.3 %collective-permute-start.5 = (bf16[256,64]{0,1:T(8,128)(2,1)S(1)}, bf16[256,64]{0,1:T(8,128)(2,1)S(1)}, u32[]{:S(2)}, u32[]{:S(2)}) collective-permute-start(bf16[256,64]{0,1:T(8,128)(2,1)S(1)} %collective-permute-done.3), channel_id=1, source_target_pairs={{0,15},{1,0},{2,1},{3,2},{4,3},{5,4},{6,5},{7,6},{8,7},{9,8},{10,9... | collective-permute-start | bytes 98312 | tf_op jit(solution)/shard_map/ppermute | solution.py:22
  20.4 0.7 collective-permute-done.4
  21.3 3.7 %collective-permute-start.7 = (bf16[256,64]{0,1:T(8,128)(2,1)S(1)}, bf16[256,64]{0,1:T(8,128)(2,1)S(1)}, u32[]{:S(2)}, u32[]{:S(2)}) collective-permute-start(bf16[256,64]{0,1:T(8,128)(2,1)S(1)} %collective-permute-done.5), channel_id=1, source_target_pairs={{0,15},{1,0},{2,1},{3,2},{4,3},{5,4},{6,5},{7,6},{8,7},{9,8},{10,9... | collective-permute-start | bytes 98312 | tf_op jit(solution)/shard_map/ppermute | solution.py:22
  25.0 0.7 collective-permute-done.6
  25.8 3.7 %collective-permute-start.9 = (bf16[256,64]{0,1:T(8,128)(2,1)S(1)}, bf16[256,64]{0,1:T(8,128)(2,1)S(1)}, u32[]{:S(2)}, u32[]{:S(2)}) collective-permute-start(bf16[256,64]{0,1:T(8,128)(2,1)S(1)} %collective-permute-done.7), channel_id=1, source_target_pairs={{0,15},{1,0},{2,1},{3,2},{4,3},{5,4},{6,5},{7,6},{8,7},{9,8},{10,9... | collective-permute-start | bytes 98312 | tf_op jit(solution)/shard_map/ppermute | solution.py:22
  29.5 0.7 collective-permute-done.8
  30.4 3.7 %collective-permute-start.11 = (bf16[256,64]{0,1:T(8,128)(2,1)S(1)}, bf16[256,64]{0,1:T(8,128)(2,1)S(1)}, u32[]{:S(2)}, u32[]{:S(2)}) collective-permute-start(bf16[256,64]{0,1:T(8,128)(2,1)S(1)} %collective-permute-done.9), channel_id=1, source_target_pairs={{0,15},{1,0},{2,1},{3,2},{4,3},{5,4},{6,5},{7,6},{8,7},{9,8},{10,9... | collective-permute-start | bytes 98312 | tf_op jit(solution)/shard_map/ppermute | solution.py:22
  34.1 0.7 collective-permute-done.10
  34.9 3.7 %collective-permute-start.13 = (bf16[256,64]{0,1:T(8,128)(2,1)S(1)}, bf16[256,64]{0,1:T(8,128)(2,1)S(1)}, u32[]{:S(2)}, u32[]{:S(2)}) collective-permute-start(bf16[256,64]{0,1:T(8,128)(2,1)S(1)} %collective-permute-done.11), channel_id=1, source_target_pairs={{0,15},{1,0},{2,1},{3,2},{4,3},{5,4},{6,5},{7,6},{8,7},{9,8},{10,9... | collective-permute-start | bytes 98312 | tf_op jit(solution)/shard_map/ppermute | solution.py:22
  38.6 0.7 collective-permute-done.12
  39.5 4.4 %collective-permute-done.14 = bf16[256,64]{0,1:T(8,128)(2,1)S(1)} collective-permute-done((bf16[256,64]{0,1:T(8,128)(2,1)S(1)}, bf16[256,64]{0,1:T(8,128)(2,1)S(1)}, u32[]{:S(2)}, u32[]{:S(2)}) %collective-permute-start.14) | collective-permute-done | bytes 32800 | tf_op jit(solution)/shard_map/ppermute | solution.py:19
  43.8 5.3 %fusion.29 = bf16[64,16,256]{2,1,0:T(8,128)(2,1)S(1)} fusion(bf16[256,64,16]{0,2,1:T(8,128)(2,1)S(1)} %bitcast.89, s32[64,256]{1,0:T(8,128)} %param.4), kind=kOutput, calls=%fused_computation.42 | convolution fusion | flops 138674176 | bytes 1114112 | tf_op jit(solution)/shard_map/mnk,kmj->nmj/dot_general | solution.py:40
  49.2 2.7 %fusion.74 = f32[1024,1024]{0,1:T(8,128)} fusion(bf16[256,1024]{0,1:T(8,128)(2,1)S(1)} %bitcast.82, bf16[256,1024]{1,0:T(8,128)(2,1)S(1)} %copy-done), kind=kOutput, calls=%fused_computation.108 | convolution fusion | flops 536870912 | bytes 5242880 | tf_op jit(solution)/shard_map/dot_general | solution.py:117
  51.9 0.8 copy-done.3
  52.7 0.6 all_to_all.42
  53.4 10.0 %all-to-all-start = ((s32[16,4,256]{2,1,0:T(4,128)}), s32[16,4,256]{2,1,0:T(4,128)S(1)}, u32[]{:S(2)}, u32[]{:S(2)}) async-start(s32[16,4,256]{2,1,0:T(4,128)} %all_to_all.42), calls=%async_computation.1 | async-start | bytes 131072 | tf_op jit(solution)/shard_map/all_to_all | solution.py:114
  63.7 7.5 %all-to-all-done = s32[16,4,256]{2,1,0:T(4,128)S(1)} async-done(((s32[16,4,256]{2,1,0:T(4,128)}), s32[16,4,256]{2,1,0:T(4,128)S(1)}, u32[]{:S(2)}, u32[]{:S(2)}) %all-to-all-start) | async-done | bytes 65568 | tf_op jit(solution)/shard_map/all_to_all | solution.py:114
  71.2 6.9 %convert_reduce_fusion = f32[4,256]{1,0:T(4,128)S(1)} fusion(s32[4,4096]{1,0:T(4,128)S(1)} %bitcast.92), kind=kLoop, calls=%fused_computation.1 | loop fusion | flops 16776192 | bytes 69632 | tf_op jit(solution)/shard_map/reduce_sum | solution.py:122
  78.1 37.9 %reduce-scatter.2.cloned.1.call-done = f32[1024,64]{0,1:T(8,128)} async-done(((f32[1024,1024]{0,1:T(8,128)}), f32[1024,64]{0,1:T(8,128)}) %reduce-scatter.2.cloned.1.call-update) | async-done | bytes 262160 | tf_op jit(solution)/shard_map/reduce_scatter | solution.py:120
  116.1 13.8 %all_to_all.60 = f32[16,8,512]{2,1,0:T(8,128)S(1)} all-to-all(f32[16,8,512]{2,1,0:T(8,128)} %bitcast.91), channel_id=1, replica_groups=mesh['rows'=16,'sub'=16] {'rows'}, dimensions={0} | all-to-all | bytes 524288 | tf_op jit(solution)/shard_map/all_to_all | solution.py:71
  130.0 10.6 %all_to_all.61 = f32[16,8,512]{2,1,0:T(8,128)} all-to-all(f32[16,8,512]{2,1,0:T(8,128)S(1)} %broadcast_in_dim.9), channel_id=1, replica_groups=mesh['rows'=16,'sub'=16] {'rows'}, dimensions={0} | all-to-all | bytes 524288 | tf_op jit(solution)/shard_map/all_to_all | solution.py:74
  140.6 43.9 %all-gather.2.cloned.1.call-done = f32[1024,1024]{1,0:T(8,128)} async-done(((f32[64,1024]{1,0:T(8,128)}), f32[1024,1024]{1,0:T(8,128)}) %all-gather.2.cloned.1.call-update) | async-done | bytes 4194320 | tf_op jit(solution)/shard_map/all_gather | solution.py:136
  184.5 3.9 %multiply_reduce_fusion = f32[]{:T(128)} fusion(f32[1024,1024]{1,0:T(8,128)} %all-gather.2.cloned.1.call-done), kind=kLoop, calls=%fused_computation.9 | loop fusion | flops 2097151 | bytes 4194308 | tf_op jit(solution)/shard_map/reduce_sum | solution.py:138
  189.1 2.9 %fusion.57 = (bf16[8,1,64,1024]{3,2,1,0:T(8,128)(2,1)S(1)}, bf16[8,1,64,1024]{3,2,1,0:T(8,128)(2,1)S(1)}, f32[8,1,64,1024]{3,2,1,0:T(8,128)S(1)}) fusion(f32[]{:T(128)S(6)} %add.243, f32[8,2,64,1024]{3,2,1,0:T(8,128)} %bitcast.76, s32[]{:T(128)S(6)} %select_n.167, s32[]{:T(128)S(6)} %select_n.168), kind=kLoop, calls=%fused_computation.69 | loop fusion | flops 2621440 | bytes 8388620 | tf_op jit(solution)/shard_map/convert_element_type | solution.py:95
  191.9 0.7 fusion.66
  192.7 0.7 fusion.65
  193.8 0.8 fusion.30
  194.6 0.4 fusion.76
  195.4 0.5 fusion.33
  195.9 1.3 fusion.67
  197.6 0.7 fusion.69
  198.4 0.5 collective-permute-start.17
  198.9 1.1 collective-permute-done.16
  200.0 0.7 fusion.68
  200.8 0.8 fusion.31
  201.5 0.4 fusion.77
  202.0 0.5 add_convert_fusion.1
  202.5 1.3 fusion.70
  204.1 0.7 fusion.72
  205.2 1.3 collective-permute-done.18
  206.5 0.7 fusion.71
  207.3 0.8 fusion.32
  208.0 0.4 fusion.78
  208.5 0.5 add_convert_fusion
  209.0 1.3 fusion.73
  210.6 0.5 fusion.75
  211.1 1.9 collective-permute-done.20
  213.0 0.5 fusion.28
  213.5 1.0 copy.43
  214.5 4.6 %all-to-all-start.3 = ((bf16[256,16,64]{0,2,1:T(8,128)(2,1)}), bf16[256,16,64]{0,2,1:T(8,128)(2,1)S(1)}, u32[]{:S(2)}, u32[]{:S(2)}) async-start(bf16[256,16,64]{0,2,1:T(8,128)(2,1)} %bitcast.23), calls=%async_computation.4 | async-start | bytes 1048576 | tf_op jit(solution)/shard_map/all_to_all | solution.py:161
  219.2 17.0 %all-to-all-done.3 = bf16[256,16,64]{0,2,1:T(8,128)(2,1)S(1)} async-done(((bf16[256,16,64]{0,2,1:T(8,128)(2,1)}), bf16[256,16,64]{0,2,1:T(8,128)(2,1)S(1)}, u32[]{:S(2)}, u32[]{:S(2)}) %all-to-all-start.3) | async-done | bytes 524320 | tf_op jit(solution)/shard_map/all_to_all | solution.py:161
  236.8 3.2 %fusion.34 = f32[256,4,16]{0,2,1:T(8,128)S(1)} fusion(bf16[4096,4,16]{0,2,1:T(8,128)(2,1)S(1)} %reshape.97, s32[4,4096]{1,0:T(4,128)S(1)} %bitcast.93), kind=kOutput, calls=%fused_computation.47 | convolution fusion | flops 138412032 | bytes 655360 | tf_op jit(solution)/shard_map/mnk,nmj->kmj/dot_general | solution.py:50
  240.6 13.3 %all_to_all.62 = f32[16,16,128]{2,1,0:T(8,128)S(1)} all-to-all(f32[16,16,128]{2,1,0:T(8,128)S(1)} %pad_maximum_fusion), channel_id=1, replica_groups=mesh['rows'=16,'sub'=16] {'rows'}, dimensions={0} | all-to-all | bytes 262144 | tf_op jit(solution)/shard_map/all_to_all | solution.py:57
  254.0 0.7 broadcast_in_dim.10
  254.6 3.5 %all-to-all-start.5 = ((f32[16,16,128]{2,1,0:T(8,128)}), f32[16,16,128]{2,1,0:T(8,128)S(1)}, u32[]{:S(2)}, u32[]{:S(2)}) async-start(f32[16,16,128]{2,1,0:T(8,128)} %broadcast_in_dim.10), calls=%async_computation.6 | async-start | bytes 262144 | tf_op jit(solution)/shard_map/all_to_all | solution.py:60
  258.3 0.7 dynamic-slice_bitcast_fusion
  259.0 5.8 %all-to-all-done.5 = f32[16,16,128]{2,1,0:T(8,128)S(1)} async-done(((f32[16,16,128]{2,1,0:T(8,128)}), f32[16,16,128]{2,1,0:T(8,128)S(1)}, u32[]{:S(2)}, u32[]{:S(2)}) %all-to-all-start.5) | async-done | bytes 131104 | tf_op jit(solution)/shard_map/all_to_all | solution.py:60
  265.2 0.7 copy.52
  (68 shorter events, 5.8 us)
Async XLA Ops:
  7.2 108.9 %reduce-scatter.2.cloned.1.call-start = ((), (), s32[]{:S(2)}) async-start(), calls=%async_computation.7 | async-start | bytes 4456448 | tf_op jit(solution)/shard_map/reduce_scatter | solution.py:120
  7.2 4.4 %collective-permute-start = (bf16[256,64]{0,1:T(8,128)(2,1)}, bf16[256,64]{0,1:T(8,128)(2,1)S(1)}, u32[]{:S(2)}, u32[]{:S(2)}) collective-permute-start(bf16[256,64]{0,1:T(8,128)(2,1)} %param.5), channel_id=1, source_target_pairs={{0,1},{1,2},{2,3},{3,4},{4,5},{5,6},{6,7},{7,8},{8,9},{9,10},{10,1... | collective-permute-start | bytes 98312 | tf_op jit(solution)/shard_map/ppermute | solution.py:19
  10.2 3.6 %collective-permute-start.1 = (bf16[256,64]{0,1:T(8,128)(2,1)}, bf16[256,64]{0,1:T(8,128)(2,1)S(1)}, u32[]{:S(2)}, u32[]{:S(2)}) collective-permute-start(bf16[256,64]{0,1:T(8,128)(2,1)} %param.5), channel_id=1, source_target_pairs={{0,15},{1,0},{2,1},{3,2},{4,3},{5,4},{6,5},{7,6},{8,7},{9,8},{10,9... | collective-permute-start | bytes 98312 | tf_op jit(solution)/shard_map/ppermute | solution.py:22
  11.6 4.9 %collective-permute-start.2 = (bf16[256,64]{0,1:T(8,128)(2,1)S(1)}, bf16[256,64]{0,1:T(8,128)(2,1)S(1)}, u32[]{:S(2)}, u32[]{:S(2)}) collective-permute-start(bf16[256,64]{0,1:T(8,128)(2,1)S(1)} %collective-permute-done), channel_id=1, source_target_pairs={{0,1},{1,2},{2,3},{3,4},{4,5},{5,6},{6,7},{7,8},{8,9},{9,10},{10,1... | collective-permute-start | bytes 98312 | tf_op jit(solution)/shard_map/ppermute | solution.py:19
  13.8 3.3 %collective-permute-start.3 = (bf16[256,64]{0,1:T(8,128)(2,1)S(1)}, bf16[256,64]{0,1:T(8,128)(2,1)S(1)}, u32[]{:S(2)}, u32[]{:S(2)}) collective-permute-start(bf16[256,64]{0,1:T(8,128)(2,1)S(1)} %collective-permute-done.1), channel_id=1, source_target_pairs={{0,15},{1,0},{2,1},{3,2},{4,3},{5,4},{6,5},{7,6},{8,7},{9,8},{10,9... | collective-permute-start | bytes 98312 | tf_op jit(solution)/shard_map/ppermute | solution.py:22
  16.5 4.6 %collective-permute-start.4 = (bf16[256,64]{0,1:T(8,128)(2,1)S(1)}, bf16[256,64]{0,1:T(8,128)(2,1)S(1)}, u32[]{:S(2)}, u32[]{:S(2)}) collective-permute-start(bf16[256,64]{0,1:T(8,128)(2,1)S(1)} %collective-permute-done.2), channel_id=1, source_target_pairs={{0,1},{1,2},{2,3},{3,4},{4,5},{5,6},{6,7},{7,8},{8,9},{9,10},{10,1... | collective-permute-start | bytes 98312 | tf_op jit(solution)/shard_map/ppermute | solution.py:19
  17.1 4.1 %collective-permute-start.5 = (bf16[256,64]{0,1:T(8,128)(2,1)S(1)}, bf16[256,64]{0,1:T(8,128)(2,1)S(1)}, u32[]{:S(2)}, u32[]{:S(2)}) collective-permute-start(bf16[256,64]{0,1:T(8,128)(2,1)S(1)} %collective-permute-done.3), channel_id=1, source_target_pairs={{0,15},{1,0},{2,1},{3,2},{4,3},{5,4},{6,5},{7,6},{8,7},{9,8},{10,9... | collective-permute-start | bytes 98312 | tf_op jit(solution)/shard_map/ppermute | solution.py:22
  21.1 4.6 %collective-permute-start.6 = (bf16[256,64]{0,1:T(8,128)(2,1)S(1)}, bf16[256,64]{0,1:T(8,128)(2,1)S(1)}, u32[]{:S(2)}, u32[]{:S(2)}) collective-permute-start(bf16[256,64]{0,1:T(8,128)(2,1)S(1)} %collective-permute-done.4), channel_id=1, source_target_pairs={{0,1},{1,2},{2,3},{3,4},{4,5},{5,6},{6,7},{7,8},{8,9},{9,10},{10,1... | collective-permute-start | bytes 98312 | tf_op jit(solution)/shard_map/ppermute | solution.py:19
  21.3 4.6 %collective-permute-start.7 = (bf16[256,64]{0,1:T(8,128)(2,1)S(1)}, bf16[256,64]{0,1:T(8,128)(2,1)S(1)}, u32[]{:S(2)}, u32[]{:S(2)}) collective-permute-start(bf16[256,64]{0,1:T(8,128)(2,1)S(1)} %collective-permute-done.5), channel_id=1, source_target_pairs={{0,15},{1,0},{2,1},{3,2},{4,3},{5,4},{6,5},{7,6},{8,7},{9,8},{10,9... | collective-permute-start | bytes 98312 | tf_op jit(solution)/shard_map/ppermute | solution.py:22
  25.6 4.6 %collective-permute-start.8 = (bf16[256,64]{0,1:T(8,128)(2,1)S(1)}, bf16[256,64]{0,1:T(8,128)(2,1)S(1)}, u32[]{:S(2)}, u32[]{:S(2)}) collective-permute-start(bf16[256,64]{0,1:T(8,128)(2,1)S(1)} %collective-permute-done.6), channel_id=1, source_target_pairs={{0,1},{1,2},{2,3},{3,4},{4,5},{5,6},{6,7},{7,8},{8,9},{9,10},{10,1... | collective-permute-start | bytes 98312 | tf_op jit(solution)/shard_map/ppermute | solution.py:19
  25.8 4.6 %collective-permute-start.9 = (bf16[256,64]{0,1:T(8,128)(2,1)S(1)}, bf16[256,64]{0,1:T(8,128)(2,1)S(1)}, u32[]{:S(2)}, u32[]{:S(2)}) collective-permute-start(bf16[256,64]{0,1:T(8,128)(2,1)S(1)} %collective-permute-done.7), channel_id=1, source_target_pairs={{0,15},{1,0},{2,1},{3,2},{4,3},{5,4},{6,5},{7,6},{8,7},{9,8},{10,9... | collective-permute-start | bytes 98312 | tf_op jit(solution)/shard_map/ppermute | solution.py:22
  30.2 4.6 %collective-permute-start.10 = (bf16[256,64]{0,1:T(8,128)(2,1)S(1)}, bf16[256,64]{0,1:T(8,128)(2,1)S(1)}, u32[]{:S(2)}, u32[]{:S(2)}) collective-permute-start(bf16[256,64]{0,1:T(8,128)(2,1)S(1)} %collective-permute-done.8), channel_id=1, source_target_pairs={{0,1},{1,2},{2,3},{3,4},{4,5},{5,6},{6,7},{7,8},{8,9},{9,10},{10,1... | collective-permute-start | bytes 98312 | tf_op jit(solution)/shard_map/ppermute | solution.py:19
  30.4 4.6 %collective-permute-start.11 = (bf16[256,64]{0,1:T(8,128)(2,1)S(1)}, bf16[256,64]{0,1:T(8,128)(2,1)S(1)}, u32[]{:S(2)}, u32[]{:S(2)}) collective-permute-start(bf16[256,64]{0,1:T(8,128)(2,1)S(1)} %collective-permute-done.9), channel_id=1, source_target_pairs={{0,15},{1,0},{2,1},{3,2},{4,3},{5,4},{6,5},{7,6},{8,7},{9,8},{10,9... | collective-permute-start | bytes 98312 | tf_op jit(solution)/shard_map/ppermute | solution.py:22
  34.7 4.6 %collective-permute-start.12 = (bf16[256,64]{0,1:T(8,128)(2,1)S(1)}, bf16[256,64]{0,1:T(8,128)(2,1)S(1)}, u32[]{:S(2)}, u32[]{:S(2)}) collective-permute-start(bf16[256,64]{0,1:T(8,128)(2,1)S(1)} %collective-permute-done.10), channel_id=1, source_target_pairs={{0,1},{1,2},{2,3},{3,4},{4,5},{5,6},{6,7},{7,8},{8,9},{9,10},{10,1... | collective-permute-start | bytes 98312 | tf_op jit(solution)/shard_map/ppermute | solution.py:19
  34.9 4.6 %collective-permute-start.13 = (bf16[256,64]{0,1:T(8,128)(2,1)S(1)}, bf16[256,64]{0,1:T(8,128)(2,1)S(1)}, u32[]{:S(2)}, u32[]{:S(2)}) collective-permute-start(bf16[256,64]{0,1:T(8,128)(2,1)S(1)} %collective-permute-done.11), channel_id=1, source_target_pairs={{0,15},{1,0},{2,1},{3,2},{4,3},{5,4},{6,5},{7,6},{8,7},{9,8},{10,9... | collective-permute-start | bytes 98312 | tf_op jit(solution)/shard_map/ppermute | solution.py:22
  39.3 4.6 %collective-permute-start.14 = (bf16[256,64]{0,1:T(8,128)(2,1)S(1)}, bf16[256,64]{0,1:T(8,128)(2,1)S(1)}, u32[]{:S(2)}, u32[]{:S(2)}) collective-permute-start(bf16[256,64]{0,1:T(8,128)(2,1)S(1)} %collective-permute-done.12), channel_id=1, source_target_pairs={{0,1},{1,2},{2,3},{3,4},{4,5},{5,6},{6,7},{7,8},{8,9},{9,10},{10,1... | collective-permute-start | bytes 98312 | tf_op jit(solution)/shard_map/ppermute | solution.py:19
  43.8 5.3 %copy-start = (bf16[256,1024]{1,0:T(8,128)(2,1)S(1)}, bf16[256,1024]{1,0:T(8,128)(2,1)}, u32[]{:S(2)}) copy-start(bf16[256,1024]{1,0:T(8,128)(2,1)} %param.3) | copy-start | bytes 1572868
  51.9 0.8 copy-start.3
  53.4 17.9 %all-to-all-start = ((s32[16,4,256]{2,1,0:T(4,128)}), s32[16,4,256]{2,1,0:T(4,128)S(1)}, u32[]{:S(2)}, u32[]{:S(2)}) async-start(s32[16,4,256]{2,1,0:T(4,128)} %all_to_all.42), calls=%async_computation.1 | async-start | bytes 131072 | tf_op jit(solution)/shard_map/all_to_all | solution.py:114
  63.4 121.1 %all-gather.2.cloned.1.call-start = ((), (), s32[]{:S(2)}) async-start(), calls=%async_computation.8 | async-start | bytes 4456448 | tf_op jit(solution)/shard_map/all_gather | solution.py:136
  193.4 2.0 collective-permute-start.15
  197.3 2.7 %collective-permute-start.16 = (bf16[512,1024]{1,0:T(8,128)(2,1)S(1)}, bf16[512,1024]{1,0:T(8,128)(2,1)S(1)}, u32[]{:S(2)}, u32[]{:S(2)}) collective-permute-start(bf16[512,1024]{1,0:T(8,128)(2,1)S(1)} %get-tuple-element.37), channel_id=1, source_target_pairs={{0,1},{1,0},{2,3},{3,2},{4,5},{5,4},{6,7},{7,6},{8,9},{9,8},{10,11... | collective-permute-start | bytes 3145736 | tf_op jit(solution)/shard_map/ppermute | solution.py:91
  198.4 3.6 %collective-permute-start.17 = (bf16[512,512]{0,1:T(8,128)(2,1)S(1)}, bf16[512,512]{0,1:T(8,128)(2,1)S(1)}, u32[]{:S(2)}, u32[]{:S(2)}) collective-permute-start(bf16[512,512]{0,1:T(8,128)(2,1)S(1)} %get-tuple-element.41), channel_id=1, source_target_pairs={{0,1},{1,0},{2,3},{3,2},{4,5},{5,4},{6,7},{7,6},{8,9},{9,8},{10,11... | collective-permute-start | bytes 1572872 | tf_op jit(solution)/shard_map/ppermute | solution.py:91
  203.8 2.7 %collective-permute-start.18 = (bf16[512,1024]{1,0:T(8,128)(2,1)S(1)}, bf16[512,1024]{1,0:T(8,128)(2,1)S(1)}, u32[]{:S(2)}, u32[]{:S(2)}) collective-permute-start(bf16[512,1024]{1,0:T(8,128)(2,1)S(1)} %get-tuple-element.43), channel_id=1, source_target_pairs={{0,1},{1,0},{2,3},{3,2},{4,5},{5,4},{6,7},{7,6},{8,9},{9,8},{10,11... | collective-permute-start | bytes 3145736 | tf_op jit(solution)/shard_map/ppermute | solution.py:91
  204.9 3.6 %collective-permute-start.19 = (bf16[512,512]{0,1:T(8,128)(2,1)S(1)}, bf16[512,512]{0,1:T(8,128)(2,1)S(1)}, u32[]{:S(2)}, u32[]{:S(2)}) collective-permute-start(bf16[512,512]{0,1:T(8,128)(2,1)S(1)} %get-tuple-element.47), channel_id=1, source_target_pairs={{0,1},{1,0},{2,3},{3,2},{4,5},{5,4},{6,7},{7,6},{8,9},{9,8},{10,11... | collective-permute-start | bytes 1572872 | tf_op jit(solution)/shard_map/ppermute | solution.py:91
  210.3 2.7 %collective-permute-start.20 = (bf16[512,1024]{1,0:T(8,128)(2,1)S(1)}, bf16[512,1024]{1,0:T(8,128)(2,1)S(1)}, u32[]{:S(2)}, u32[]{:S(2)}) collective-permute-start(bf16[512,1024]{1,0:T(8,128)(2,1)S(1)} %get-tuple-element.49), channel_id=1, source_target_pairs={{0,1},{1,0},{2,3},{3,2},{4,5},{5,4},{6,7},{7,6},{8,9},{9,8},{10,11... | collective-permute-start | bytes 3145736 | tf_op jit(solution)/shard_map/ppermute | solution.py:91
  213.5 1.0 copy-start.1
  214.5 21.8 %all-to-all-start.3 = ((bf16[256,16,64]{0,2,1:T(8,128)(2,1)}), bf16[256,16,64]{0,2,1:T(8,128)(2,1)S(1)}, u32[]{:S(2)}, u32[]{:S(2)}) async-start(bf16[256,16,64]{0,2,1:T(8,128)(2,1)} %bitcast.23), calls=%async_computation.4 | async-start | bytes 1048576 | tf_op jit(solution)/shard_map/all_to_all | solution.py:161
  240.0 18.1 %copy-start.2 = (bf16[256,64]{0,1:T(8,128)(2,1)S(1)}, bf16[256,64]{0,1:T(8,128)(2,1)}, u32[]{:S(2)}) copy-start(bf16[256,64]{0,1:T(8,128)(2,1)} %param.5) | copy-start | bytes 98308
  254.6 10.2 %all-to-all-start.5 = ((f32[16,16,128]{2,1,0:T(8,128)}), f32[16,16,128]{2,1,0:T(8,128)S(1)}, u32[]{:S(2)}, u32[]{:S(2)}) async-start(f32[16,16,128]{2,1,0:T(8,128)} %broadcast_in_dim.10), calls=%async_computation.6 | async-start | bytes 262144 | tf_op jit(solution)/shard_map/all_to_all | solution.py:60
Sparse Core Ops, SparseCore 0:
  52.1 63.9 reduce-scatter.1
  140.7 43.7 all-gather.1
